TPU v7x, 256 devices: a whole 4x4x8 slice. The times are simulated.
256 devices in a mesh: seq: 32 (over y, x, z_lo), tp: 8 (over z_hi, core).
Axes of the slice: x: 4, y: 4, z: 8 (z_hi: 4, z_lo: 2; z = z_hi * 2 + z_lo), core: 2. Of those that a mesh axis runs over, the one named last changes fastest.
Arguments:
- tokens: bfloat16 [32768, 2048], P('seq'), may hold values from -20 to 20
- w_query: bfloat16 [2048, 2048], P(None, 'tp'), may hold values from -0.15467961 to 0.15467961
- w_kv: bfloat16 [2048, 512], replicated, may hold values from -0.110485435 to 0.110485435
- w_out: bfloat16 [2048, 2048], P('tp'), may hold values from -6 to 6
- seg_start: int32 [32768], P('seq'), may hold values from 0 to 32752, as said below
- page_owner: int32 [2048], replicated, may hold values from 0 to 31, as said below
- page_slot: int32 [2048], replicated, may hold values from 0 to 127, as said below
Outputs:
- layer_out: bfloat16 [32768, 2048], P('seq', 'tp')
- kv_cache: bfloat16 [65536, 512], P('seq', 'tp')
Inputs may be any that keep to these rules, and one draw needn't show every extreme that they name: seg_start[t] is the first position of the prompt that holds token t: it never falls along the stream, is a multiple of 16, is at most t, and equals t at each prompt's first token; the last page begins a prompt. `page_owner`: among the 64 pages of one stream block no owner is named more than 4 times; one owner is named exactly 4 times by the pages of every block. `page_slot`: pages with the same owner have distinct slots.
All inputs are finite; a program needn't handle non-finite values.
Results may differ from a plain program's by a relative error of at most 0.015.
Values may be sent and summed in bfloat16 or wider, within the bound.
No kernel may reach another device: no remote copies, remote signals or barrier semaphores. Data moves between devices by JAX's collectives and lax.ppermute only.
A program may use at most 64 MiB of HBM per device.

v0:
```python
import jax
import jax.numpy as jnp
from jax import lax
from jax.sharding import PartitionSpec as P

H = 32
KVH = 4
HD = 64
WINDOW = 2048
PAGE = 16
masked_value = -1e30


def passed_along(value, axis, steps):
    count = lax.axis_size(axis)
    leading, last = (max(0, -steps), min(count, count - steps))
    return lax.ppermute(value, axis, [(source, source + steps) for source in range(leading, last)])


def attend_band(query_block, band_block, positions_q, positions_k, starts):
    keys_block = band_block[:, :, 0, :]
    values_block = band_block[:, :, 1, :]
    head_size = query_block.shape[-1]
    scores = jnp.einsum(
        "qkgd,ckd->kgqc", query_block, keys_block, preferred_element_type=jnp.float32
    ) * head_size ** (-0.5)
    lower_bound = jnp.maximum(starts, positions_q - WINDOW + 1)
    visible = (positions_k[None, :] >= lower_bound[:, None]) & (
        positions_k[None, :] <= positions_q[:, None]
    )
    scores = jnp.where(visible, scores, masked_value)
    largest = jnp.max(scores, axis=-1, keepdims=True)
    powered = jnp.exp(scores - largest)
    row_total = jnp.sum(powered, axis=-1, keepdims=True)
    weights = powered.astype(jnp.bfloat16)
    result = (
        jnp.einsum("kgqc,ckd->kgqd", weights, values_block, preferred_element_type=jnp.float32)
        / row_total
    )
    return jnp.transpose(result, (2, 0, 1, 3)).astype(jnp.bfloat16)


def body(tokens, w_query, w_kv, w_out, seg_start, page_owner, page_slot):
    seq_index = lax.axis_index("seq")
    tp_index = lax.axis_index("tp")
    seq_count = lax.axis_size("seq")
    tp_count = lax.axis_size("tp")
    tok_rows = tokens.shape[0]
    group_size = H // KVH
    heads_dev = H // tp_count
    kv_heads_dev = max(1, heads_dev // group_size)
    kv_width = kv_heads_dev * 2 * HD
    cache_width = KVH * 2 * HD // tp_count
    first_col = tp_index * heads_dev // group_size * 2 * HD
    queries = jnp.dot(tokens, w_query, preferred_element_type=jnp.float32).astype(jnp.bfloat16)
    w_local = lax.dynamic_slice_in_dim(w_kv, first_col, kv_width, 1)
    key_value = jnp.dot(tokens, w_local, preferred_element_type=jnp.float32).astype(jnp.bfloat16)
    own_cols = lax.dynamic_slice_in_dim(
        key_value, tp_index * cache_width - first_col, cache_width, 1
    )
    pages_dev = tok_rows // PAGE
    slots_per = max(2, 2 * pages_dev // seq_count)
    cache_slots = seq_count * slots_per
    owners_all = page_owner.reshape(seq_count, pages_dev)
    owner_hot = (
        owners_all[:, :, None] == jnp.arange(seq_count, dtype=jnp.int32)[None, None, :]
    ).astype(jnp.int32)
    local_rank = jnp.sum((jnp.cumsum(owner_hot, axis=1) - owner_hot) * owner_hot, axis=2)
    column_of = jnp.arange(seq_count, dtype=jnp.int32)[:, None] * slots_per + local_rank
    own_owner = lax.dynamic_index_in_dim(owners_all, seq_index, 0, keepdims=False)
    own_rank = lax.dynamic_index_in_dim(local_rank, seq_index, 0, keepdims=False)
    destination = own_owner * slots_per + own_rank
    send_table = (jnp.arange(cache_slots, dtype=jnp.int32)[:, None] == destination[None, :]).astype(
        jnp.bfloat16
    )
    page_rows = own_cols.reshape(pages_dev, PAGE * cache_width)
    outgoing_pages = jnp.dot(send_table, page_rows, preferred_element_type=jnp.float32).astype(
        jnp.bfloat16
    )
    outgoing_pages = outgoing_pages.reshape(seq_count, slots_per, PAGE * cache_width)
    arrived = lax.all_to_all(outgoing_pages, "seq", split_axis=0, concat_axis=0, tiled=True)
    owned_here = page_owner == seq_index
    place_table = (
        (page_slot[None, :] == jnp.arange(cache_slots, dtype=jnp.int32)[:, None])
        & owned_here[None, :]
    ).astype(jnp.bfloat16)
    pick_table = (
        column_of.reshape(-1)[:, None] == jnp.arange(cache_slots, dtype=jnp.int32)[None, :]
    ).astype(jnp.bfloat16)
    route_table = jnp.dot(place_table, pick_table, preferred_element_type=jnp.float32).astype(
        jnp.bfloat16
    )
    cache_local = jnp.dot(
        route_table,
        arrived.reshape(cache_slots, PAGE * cache_width),
        preferred_element_type=jnp.float32,
    )
    kv_cache = cache_local.astype(jnp.bfloat16).reshape(cache_slots * PAGE, cache_width)
    blocks_back = WINDOW // tok_rows
    pieces = []
    for distance in range(blocks_back, 0, -1):
        pieces.append(passed_along(key_value, "seq", distance))
    behind = jnp.concatenate(pieces, axis=0)
    band_all = jnp.concatenate([behind, key_value], axis=0).reshape(-1, kv_heads_dev, 2, HD)
    query_heads = queries.reshape(tok_rows, kv_heads_dev, heads_dev // kv_heads_dev, HD)
    block_rows = min(256, tok_rows)
    base_position = seq_index * tok_rows

    def one_block(block_idx):
        first_row = block_idx * block_rows
        query_block = lax.dynamic_slice_in_dim(query_heads, first_row, block_rows, 0)
        band_block = lax.dynamic_slice_in_dim(band_all, first_row, WINDOW + block_rows, 0)
        starts = lax.dynamic_slice_in_dim(seg_start, first_row, block_rows, 0)
        positions_q = base_position + first_row + jnp.arange(block_rows, dtype=jnp.int32)
        positions_k = (
            base_position + first_row - WINDOW + jnp.arange(WINDOW + block_rows, dtype=jnp.int32)
        )
        return attend_band(query_block, band_block, positions_q, positions_k, starts)

    attended = lax.map(one_block, jnp.arange(tok_rows // block_rows, dtype=jnp.int32))
    attended = attended.reshape(tok_rows, heads_dev * HD)
    projected = jnp.dot(attended, w_out, preferred_element_type=jnp.float32)
    summed = lax.psum(projected.astype(jnp.bfloat16), "tp").astype(jnp.float32)
    width_dev = summed.shape[1] // tp_count
    layer_out = lax.dynamic_slice_in_dim(summed, tp_index * width_dev, width_dev, 1).astype(
        jnp.bfloat16
    )
    return (layer_out, kv_cache)


def solution(mesh):
    return jax.shard_map(
        body,
        mesh=mesh,
        in_specs=(P("seq", None), P(None, "tp"), P(), P("tp", None), P("seq"), P(), P()),
        out_specs=(P("seq", "tp"), P("seq", "tp")),
        check_vma=False,
    )
```

profile of v0, /device:TPU:65, one launch (start us, length us, event | category | flops | bytes accessed | tf_op | source)
XLA Modules:
  0.0 213.9 jit_solution(16457602136221309663)
XLA Ops:
  8.8 3.7 %convolution_convert_fusion.4 = bf16[128,1024]{1,0:T(8,128)(2,1)S(1)} fusion(bf16[1024,2048]{1,0:T(8,128)(2,1)} %param.9, bf16[2048,512]{1,0:T(8,128)(2,1)S(1)} %copy-done, s32[]{:T(128)S(6)} %select_n.52), kind=kOutput, calls=%fused_computation.32 | convolution fusion | flops 537001984 | bytes 4980740 | tf_op jit(solution)/shard_map/dot_general | solution.py:57
  12.5 3.6 %collective-permute-start.1 = (bf16[1024,128]{0,1:T(8,128)(2,1)S(1)}, bf16[1024,128]{0,1:T(8,128)(2,1)S(1)}, u32[]{:S(2)}, u32[]{:S(2)}) collective-permute-start(bf16[1024,128]{0,1:T(8,128)(2,1)S(1)} %bitcast.95), channel_id=1, source_target_pairs={{0,8},{8,16},{16,24},{24,32},{32,40},{40,48},{48,56},{56,64},{64,7... | collective-permute-start | bytes 786440 | tf_op jit(solution)/shard_map/ppermute | solution.py:17
  16.1 3.1 %collective-permute-start = (bf16[1024,128]{0,1:T(8,128)(2,1)S(1)}, bf16[1024,128]{0,1:T(8,128)(2,1)S(1)}, u32[]{:S(2)}, u32[]{:S(2)}) collective-permute-start(bf16[1024,128]{0,1:T(8,128)(2,1)S(1)} %bitcast.96), channel_id=1, source_target_pairs={{0,16},{8,24},{16,32},{24,40},{32,48},{40,56},{48,64},{56,72},{64,... | collective-permute-start | bytes 786440 | tf_op jit(solution)/shard_map/ppermute | solution.py:17
  19.2 4.6 %convolution_convert_fusion.1 = bf16[1024,256]{0,1:T(8,128)(2,1)} fusion(bf16[1024,2048]{1,0:T(8,128)(2,1)} %param.9, bf16[2048,256]{1,0:T(8,128)(2,1)} %param.10), kind=kOutput, calls=%fused_computation.29 | convolution fusion | flops 1074003968 | bytes 5767168 | tf_op jit(solution)/shard_map/dot_general | solution.py:55
  23.8 4.3 %collective-permute-done = bf16[1024,128]{0,1:T(8,128)(2,1)S(1)} collective-permute-done((bf16[1024,128]{0,1:T(8,128)(2,1)S(1)}, bf16[1024,128]{0,1:T(8,128)(2,1)S(1)}, u32[]{:S(2)}, u32[]{:S(2)}) %collective-permute-start) | collective-permute-done | bytes 262176 | tf_op jit(solution)/shard_map/ppermute | solution.py:17
  29.1 47.1 %while.15 = (s32[]{:T(128)}, bf16[4,256,1,4,64]{1,4,3,2,0:T(8,128)(2,1)}, s32[4]{0:T(128)S(1)}, s32[]{:T(128)}, s32[1024]{0:T(1024)}, /*index=5*/bf16[3072,1,2,6...) while((s32[]{:T(128)}, ...), condition=%wide.region_3.4_spmd, body=%wide.region_0.0_spmd.sunk | while | flops 631833600 | bytes 31567140 | solution.py:120
  32.2 2.6 %fusion.55 = (f32[4,256]{1,0:T(4,128)S(1)}, f32[2304,256,4]{1,0,2:T(8,128)S(1)}) fusion(pred[256,2304]{0,1:T(8,128)(4,1)S(1)} %compare_and_fusion.2, bf16[1024,1,4,64]{0,3,2,1:T(8,128)(2,1)} %get-tuple-element.277, s32[]{:T(128)S(6)} %select_n.82, bf16[3072,1,2,64]{0,3,2,1:T(8,128)(2,1)} %get-tuple-element.276, s32[]{:T(128)S(6)} %select_n.83), kind=kOutput, calls=%fused_computation.4.clone.1 | convolution fusion | flops 309066752 | bytes 10457096 | tf_op jit(solution)/shard_map/while/body/eval_jaxpr/qkgd,ckd->kgqc/dot_general | solution.py:24
  34.8 2.0 fusion.56
  36.8 4.1 %fusion.57 = bf16[4,256,1,4,64]{1,4,3,2,0:T(8,128)(2,1)} fusion(bf16[4,256,1,4,64]{1,4,3,2,0:T(8,128)(2,1)} %get-tuple-element.258, s32[]{:T(128)S(6)} %copy.40, f32[2304,256,4]{1,0,2:T(8,128)S(1)} %get-tuple-element.241, f32[4,256]{1,0:T(4,128)S(1)} %get-tuple-element.242, pred[256,2304]{0,1:T(8,128)(4,1)S(1)} %compare_and_fusion.2, ...), kind=kOutput, calls=%fused_computation.12.clone.1 | convolution fusion | flops 311558144 | bytes 10461196 | tf_op jit(solution)/shard_map/while/body/eval_jaxpr/kgqc,ckd->kgqd/dot_general | solution.py:37
  43.9 2.6 %fusion.55 = (f32[4,256]{1,0:T(4,128)S(1)}, f32[2304,256,4]{1,0,2:T(8,128)S(1)}) fusion(pred[256,2304]{0,1:T(8,128)(4,1)S(1)} %compare_and_fusion.2, bf16[1024,1,4,64]{0,3,2,1:T(8,128)(2,1)} %get-tuple-element.277, s32[]{:T(128)S(6)} %select_n.82, bf16[3072,1,2,64]{0,3,2,1:T(8,128)(2,1)} %get-tuple-element.276, s32[]{:T(128)S(6)} %select_n.83), kind=kOutput, calls=%fused_computation.4.clone.1 | convolution fusion | flops 309066752 | bytes 10457096 | tf_op jit(solution)/shard_map/while/body/eval_jaxpr/qkgd,ckd->kgqc/dot_general | solution.py:24
  46.6 2.0 fusion.56
  48.6 4.1 %fusion.57 = bf16[4,256,1,4,64]{1,4,3,2,0:T(8,128)(2,1)} fusion(bf16[4,256,1,4,64]{1,4,3,2,0:T(8,128)(2,1)} %get-tuple-element.258, s32[]{:T(128)S(6)} %copy.40, f32[2304,256,4]{1,0,2:T(8,128)S(1)} %get-tuple-element.241, f32[4,256]{1,0:T(4,128)S(1)} %get-tuple-element.242, pred[256,2304]{0,1:T(8,128)(4,1)S(1)} %compare_and_fusion.2, ...), kind=kOutput, calls=%fused_computation.12.clone.1 | convolution fusion | flops 311558144 | bytes 10461196 | tf_op jit(solution)/shard_map/while/body/eval_jaxpr/kgqc,ckd->kgqd/dot_general | solution.py:37
  55.7 2.6 %fusion.55 = (f32[4,256]{1,0:T(4,128)S(1)}, f32[2304,256,4]{1,0,2:T(8,128)S(1)}) fusion(pred[256,2304]{0,1:T(8,128)(4,1)S(1)} %compare_and_fusion.2, bf16[1024,1,4,64]{0,3,2,1:T(8,128)(2,1)} %get-tuple-element.277, s32[]{:T(128)S(6)} %select_n.82, bf16[3072,1,2,64]{0,3,2,1:T(8,128)(2,1)} %get-tuple-element.276, s32[]{:T(128)S(6)} %select_n.83), kind=kOutput, calls=%fused_computation.4.clone.1 | convolution fusion | flops 309066752 | bytes 10457096 | tf_op jit(solution)/shard_map/while/body/eval_jaxpr/qkgd,ckd->kgqc/dot_general | solution.py:24
  58.3 2.0 fusion.56
  60.3 4.1 %fusion.57 = bf16[4,256,1,4,64]{1,4,3,2,0:T(8,128)(2,1)} fusion(bf16[4,256,1,4,64]{1,4,3,2,0:T(8,128)(2,1)} %get-tuple-element.258, s32[]{:T(128)S(6)} %copy.40, f32[2304,256,4]{1,0,2:T(8,128)S(1)} %get-tuple-element.241, f32[4,256]{1,0:T(4,128)S(1)} %get-tuple-element.242, pred[256,2304]{0,1:T(8,128)(4,1)S(1)} %compare_and_fusion.2, ...), kind=kOutput, calls=%fused_computation.12.clone.1 | convolution fusion | flops 311558144 | bytes 10461196 | tf_op jit(solution)/shard_map/while/body/eval_jaxpr/kgqc,ckd->kgqd/dot_general | solution.py:37
  67.5 2.6 %fusion.55 = (f32[4,256]{1,0:T(4,128)S(1)}, f32[2304,256,4]{1,0,2:T(8,128)S(1)}) fusion(pred[256,2304]{0,1:T(8,128)(4,1)S(1)} %compare_and_fusion.2, bf16[1024,1,4,64]{0,3,2,1:T(8,128)(2,1)} %get-tuple-element.277, s32[]{:T(128)S(6)} %select_n.82, bf16[3072,1,2,64]{0,3,2,1:T(8,128)(2,1)} %get-tuple-element.276, s32[]{:T(128)S(6)} %select_n.83), kind=kOutput, calls=%fused_computation.4.clone.1 | convolution fusion | flops 309066752 | bytes 10457096 | tf_op jit(solution)/shard_map/while/body/eval_jaxpr/qkgd,ckd->kgqc/dot_general | solution.py:24
  70.1 2.0 fusion.56
  72.1 4.1 %fusion.57 = bf16[4,256,1,4,64]{1,4,3,2,0:T(8,128)(2,1)} fusion(bf16[4,256,1,4,64]{1,4,3,2,0:T(8,128)(2,1)} %get-tuple-element.258, s32[]{:T(128)S(6)} %copy.40, f32[2304,256,4]{1,0,2:T(8,128)S(1)} %get-tuple-element.241, f32[4,256]{1,0:T(4,128)S(1)} %get-tuple-element.242, pred[256,2304]{0,1:T(8,128)(4,1)S(1)} %compare_and_fusion.2, ...), kind=kOutput, calls=%fused_computation.12.clone.1 | convolution fusion | flops 311558144 | bytes 10461196 | tf_op jit(solution)/shard_map/while/body/eval_jaxpr/kgqc,ckd->kgqd/dot_general | solution.py:37
  77.7 3.3 %convolution_convert_fusion = bf16[1024,2048]{1,0:T(8,128)(2,1)} fusion(bf16[1024,256]{0,1:T(8,128)(2,1)S(1)} %bitcast.93, bf16[256,2048]{1,0:T(8,128)(2,1)S(1)} %copy-done.1), kind=kOutput, calls=%fused_computation.25 | convolution fusion | flops 1075838976 | bytes 5767168 | tf_op jit(solution)/shard_map/dot_general | solution.py:122
  81.6 1.7 select_reduce_fusion
  84.6 8.0 %all-to-all-start = ((bf16[32,4,1024]{2,1,0:T(4,128)(2,1)}), bf16[32,4,1024]{2,1,0:T(4,128)(2,1)S(1)}, u32[]{:S(2)}, u32[]{:S(2)}) async-start(bf16[32,4,1024]{2,1,0:T(4,128)(2,1)} %reshape.133), calls=%async_computation | async-start | bytes 524288 | tf_op jit(solution)/shard_map/all_to_all | solution.py:81
  92.8 8.5 %all-to-all-done = bf16[32,4,1024]{2,1,0:T(4,128)(2,1)S(1)} async-done(((bf16[32,4,1024]{2,1,0:T(4,128)(2,1)}), bf16[32,4,1024]{2,1,0:T(4,128)(2,1)S(1)}, u32[]{:S(2)}, u32[]{:S(2)}) %all-to-all-start) | async-done | bytes 262176 | tf_op jit(solution)/shard_map/all_to_all | solution.py:81
  103.4 101.8 %all-reduce.2.cloned.1.call-done = bf16[1024,2048]{1,0:T(8,128)(2,1)} async-done(((bf16[1024,2048]{1,0:T(8,128)(2,1)}), bf16[1024,2048]{1,0:T(8,128)(2,1)}) %all-reduce.2.cloned.1.call-update) | async-done | bytes 4194320 | tf_op jit(solution)/shard_map/psum | solution.py:123
  205.2 1.9 convert_convert_fusion
  (49 shorter events, 17.8 us)
Async XLA Ops:
  7.2 1.6 copy-start
  7.2 198.0 %all-reduce.2.cloned.1.call-start = ((), (), s32[]{:S(2)}) async-start(), calls=%async_computation.1 | async-start | bytes 8388608 | tf_op jit(solution)/shard_map/psum | solution.py:123
  12.5 11.3 %collective-permute-start.1 = (bf16[1024,128]{0,1:T(8,128)(2,1)S(1)}, bf16[1024,128]{0,1:T(8,128)(2,1)S(1)}, u32[]{:S(2)}, u32[]{:S(2)}) collective-permute-start(bf16[1024,128]{0,1:T(8,128)(2,1)S(1)} %bitcast.95), channel_id=1, source_target_pairs={{0,8},{8,16},{16,24},{24,32},{32,40},{40,48},{48,56},{56,64},{64,7... | collective-permute-start | bytes 786440 | tf_op jit(solution)/shard_map/ppermute | solution.py:17
  16.1 12.1 %collective-permute-start = (bf16[1024,128]{0,1:T(8,128)(2,1)S(1)}, bf16[1024,128]{0,1:T(8,128)(2,1)S(1)}, u32[]{:S(2)}, u32[]{:S(2)}) collective-permute-start(bf16[1024,128]{0,1:T(8,128)(2,1)S(1)} %bitcast.96), channel_id=1, source_target_pairs={{0,16},{8,24},{16,32},{24,40},{32,48},{40,56},{48,64},{56,72},{64,... | collective-permute-start | bytes 786440 | tf_op jit(solution)/shard_map/ppermute | solution.py:17
  29.1 48.6 %copy-start.1 = (bf16[256,2048]{1,0:T(8,128)(2,1)S(1)}, bf16[256,2048]{1,0:T(8,128)(2,1)}, u32[]{:S(2)}) copy-start(bf16[256,2048]{1,0:T(8,128)(2,1)} %param.12) | copy-start | bytes 3145732
  77.7 3.3 %copy-start.2 = (s32[2048]{0:T(1024)S(1)}, s32[2048]{0:T(1024)}, u32[]{:S(2)}) copy-start(s32[2048]{0:T(1024)} %param.14) | copy-start | bytes 24580
  81.0 20.4 %copy-start.3 = (s32[2048]{0:T(1024)S(1)}, s32[2048]{0:T(1024)}, u32[]{:S(2)}) copy-start(s32[2048]{0:T(1024)} %param.15) | copy-start | bytes 24580
  84.6 16.8 %all-to-all-start = ((bf16[32,4,1024]{2,1,0:T(4,128)(2,1)}), bf16[32,4,1024]{2,1,0:T(4,128)(2,1)S(1)}, u32[]{:S(2)}, u32[]{:S(2)}) async-start(bf16[32,4,1024]{2,1,0:T(4,128)(2,1)} %reshape.133), calls=%async_computation | async-start | bytes 524288 | tf_op jit(solution)/shard_map/all_to_all | solution.py:81
Sparse Core Ops, SparseCore 0:
  81.2 124.0 all-reduce.1
where the time goes:
time: 215 us; the launch traced here: 214 us
  waiting for transfers between devices  115 us (53%)
  matrix products  39.2 us (18%)
  other arithmetic  20.2 us (9%)
  starting transfers between devices  14.7 us (7%)
  between operations  14.2 us (7%)
  local copies, waits for them, and re-layouts  8.25 us (4%)
  loops' own time  2.64 us (1%)
    psum x1, waiting for transfers between devices, body(): summed = lax.psum(projected.astype(jnp.bfloat16), 'tp').astype(jnp.float32)  102 us
    dot_general x4, matrix products, attend_band(): jnp.einsum('kgqc,ckd->kgqd', weights, values_block, preferred_element_typ...  16.3 us
    dot_general x4, matrix products, attend_band(): jnp.einsum('qkgd,ckd->kgqc', query_block, keys_block, preferred_element_t...  10.4 us
    all_to_all x1, waiting for transfers between devices, body(): lax.all_to_all(outgoing_pages, 'seq', split_axis=0, concat_axis=0, tiled=...  8.51 us
    all_to_all x1, starting transfers between devices, body(): lax.all_to_all(outgoing_pages, 'seq', split_axis=0, concat_axis=0, tiled=...  8.02 us
    reduce_sum x4, other arithmetic, attend_band(): row_total = jnp.sum(powered, axis=-1, keepdims=True)  7.98 us
    ppermute x2, starting transfers between devices, passed_along(): lax.ppermute(value, axis, [(source, source + steps) for source in range(l...  6.68 us
    dot_general x1, matrix products, body(): jnp.dot(tokens, w_query, preferred_element_type=jnp.float32)  4.58 us
  transfers between devices with their start and end apart: 4, of which 3 were waited for; matrix products, arithmetic and copies ran while one was open for 5% of the time, Pallas kernels for 0%

commit v1 on v0

--- a/solution.py
+++ b/solution.py
@@ -1,3 +1,4 @@
+import functools
 import jax
 import jax.numpy as jnp
 from jax import lax
@@ -9,6 +10,13 @@
 WINDOW = 2048
 PAGE = 16
 masked_value = -1e30
+
+
+def feed_the_core(raw, link_axis):
+    return jnp.sum(lax.all_gather(raw, axis_name=link_axis), axis=0)
+
+
+_resolve_waves = functools.partial(feed_the_core, link_axis="tp")
 
 
 def passed_along(value, axis, steps):
@@ -120,7 +128,7 @@
     attended = lax.map(one_block, jnp.arange(tok_rows // block_rows, dtype=jnp.int32))
     attended = attended.reshape(tok_rows, heads_dev * HD)
     projected = jnp.dot(attended, w_out, preferred_element_type=jnp.float32)
-    summed = lax.psum(projected.astype(jnp.bfloat16), "tp").astype(jnp.float32)
+    summed = _resolve_waves(projected.astype(jnp.bfloat16)).astype(jnp.float32)
     width_dev = summed.shape[1] // tp_count
     layer_out = lax.dynamic_slice_in_dim(summed, tp_index * width_dev, width_dev, 1).astype(
         jnp.bfloat16

time: 215 us -> 395 us (1.84); the launches traced: 214 us -> 388 us
  waiting for transfers between devices: 115 us -> 287 us
  other arithmetic: 20.2 us -> 33.6 us
  matrix products: 39.2 us -> 27.9 us
    all_gather x0 -> x1, waiting for transfers between devices: none -> 273 us  [feed_the_core(): return jnp.sum(lax.all_gather(raw, axis_name=link_axis), axis=0)]
    psum x1 -> x0, waiting for transfers between devices: 102 us -> none  [body(): summed = lax.psum(projected.astype(jnp.bfloat16), 'tp').astype(jnp.float32)]
    reduce_sum x0 -> x1, other arithmetic: none -> 14.3 us  [feed_the_core(): return jnp.sum(lax.all_gather(raw, axis_name=link_axis), axis=0)]
    dot_general x4, matrix products: 16.3 us -> 9.47 us  [attend_band(): jnp.einsum('kgqc,ckd->kgqd', weights, values_block, preferred_element_typ...]
  transfers between devices with their start and end apart: 4 -> 4, of which waited for: 3 -> 3; matrix products, arithmetic and copies ran while one was open for 5% -> 2% of each run, Pallas kernels for 0% -> 0%
where the time goes in v1:
time: 395 us; the launch traced here: 388 us
  waiting for transfers between devices  287 us (73%)
  other arithmetic  33.6 us (9%)
  matrix products  27.9 us (7%)
  starting transfers between devices  14.7 us (4%)
  between operations  14.3 us (4%)
  local copies, waits for them, and re-layouts  7.49 us (2%)
    all_gather x1, waiting for transfers between devices, feed_the_core(): return jnp.sum(lax.all_gather(raw, axis_name=link_axis), axis=0)  273 us
    reduce_sum x1, other arithmetic, feed_the_core(): return jnp.sum(lax.all_gather(raw, axis_name=link_axis), axis=0)  14.3 us
    dot_general x4, matrix products, attend_band(): jnp.einsum('kgqc,ckd->kgqd', weights, values_block, preferred_element_typ...  9.47 us
    all_to_all x1, waiting for transfers between devices, body(): lax.all_to_all(outgoing_pages, 'seq', split_axis=0, concat_axis=0, tiled=...  8.5 us
    reduce_sum x4, other arithmetic, attend_band(): row_total = jnp.sum(powered, axis=-1, keepdims=True)  8.04 us
    all_to_all x1, starting transfers between devices, body(): lax.all_to_all(outgoing_pages, 'seq', split_axis=0, concat_axis=0, tiled=...  8.02 us
  transfers between devices with their start and end apart: 4, of which 3 were waited for; matrix products, arithmetic and copies ran while one was open for 2% of the time, Pallas kernels for 0%

profile of v1, /device:TPU:65, one launch (start us, length us, event | category | flops | bytes accessed | tf_op | source)
XLA Modules:
  0.0 387.6 jit_solution(18393237024506932194)
XLA Ops:
  8.8 3.7 convolution_convert_fusion.4
  12.5 3.6 collective-permute-start.1
  16.1 3.1 collective-permute-start
  19.2 3.8 convolution_convert_fusion.1
  23.0 5.1 %collective-permute-done = bf16[1024,128]{0,1:T(8,128)(2,1)S(1)} collective-permute-done((bf16[1024,128]{0,1:T(8,128)(2,1)S(1)}, bf16[1024,128]{0,1:T(8,128)(2,1)S(1)}, u32[]{:S(2)}, u32[]{:S(2)}) %collective-permute-start) | collective-permute-done | bytes 262176 | tf_op jit(solution)/shard_map/ppermute | solution.py:25
  28.2 37.1 %while.15 = (s32[]{:T(128)}, bf16[4,256,1,4,64]{1,4,3,2,0:T(8,128)(2,1)S(1)}, s32[4]{0:T(128)S(1)}, s32[]{:T(128)}, s32[1024]{0:T(1024)}, /*index=5*/bf16[3072,1...) while((s32[]{:T(128)}, ...), condition=%wide.region_3.4_spmd, body=%wide.region_0.0_spmd.sunk | while | flops 631833600 | bytes 31567140 | solution.py:128
  31.5 1.7 fusion.55
  33.1 2.0 fusion.56
  35.1 2.4 fusion.57
  40.8 1.7 fusion.55
  42.4 2.0 fusion.56
  44.4 2.4 fusion.57
  50.0 1.7 fusion.55
  51.7 2.0 fusion.56
  53.7 2.4 fusion.57
  61.0 2.0 fusion.56
  63.0 2.4 fusion.57
  65.9 3.3 convolution_convert_fusion
  69.9 1.7 select_reduce_fusion
  72.8 8.0 %all-to-all-start = ((bf16[32,4,1024]{2,1,0:T(4,128)(2,1)}), bf16[32,4,1024]{2,1,0:T(4,128)(2,1)S(1)}, u32[]{:S(2)}, u32[]{:S(2)}) async-start(bf16[32,4,1024]{2,1,0:T(4,128)(2,1)} %reshape.133), calls=%async_computation | async-start | bytes 524288 | tf_op jit(solution)/shard_map/all_to_all | solution.py:89
  81.0 8.5 %all-to-all-done = bf16[32,4,1024]{2,1,0:T(4,128)(2,1)S(1)} async-done(((bf16[32,4,1024]{2,1,0:T(4,128)(2,1)}), bf16[32,4,1024]{2,1,0:T(4,128)(2,1)S(1)}, u32[]{:S(2)}, u32[]{:S(2)}) %all-to-all-start) | async-done | bytes 262176 | tf_op jit(solution)/shard_map/all_to_all | solution.py:89
  91.6 273.0 %all-gather.3.cloned.1.call-done = bf16[8192,2048]{1,0:T(8,128)(2,1)} async-done(((bf16[1024,2048]{1,0:T(8,128)(2,1)}), bf16[8192,2048]{1,0:T(8,128)(2,1)}) %all-gather.3.cloned.1.call-update) | async-done | bytes 33554448 | tf_op jit(solution)/shard_map/all_gather | solution.py:16
  364.6 14.3 %reduce_sum.30 = bf16[1024,2048]{1,0:T(8,128)(2,1)} reduce(bf16[8,1024,2048]{2,1,0:T(8,128)(2,1)} %bitcast.94, bf16[]{:T(256)} %constant.147.clone.1), dimensions={0}, to_apply=%region_4.5 | reduce | flops 14680064 | bytes 37748736 | tf_op jit(solution)/shard_map/reduce_sum | solution.py:16
  378.9 1.9 convert_convert_fusion
  (52 shorter events, 17.9 us)
Async XLA Ops:
  7.2 1.6 copy-start
  7.2 357.4 %all-gather.3.cloned.1.call-start = ((), (), s32[]{:S(2)}) async-start(), calls=%async_computation.1 | async-start | bytes 37748736 | tf_op jit(solution)/shard_map/all_gather | solution.py:16
  12.5 10.5 %collective-permute-start.1 = (bf16[1024,128]{0,1:T(8,128)(2,1)S(1)}, bf16[1024,128]{0,1:T(8,128)(2,1)S(1)}, u32[]{:S(2)}, u32[]{:S(2)}) collective-permute-start(bf16[1024,128]{0,1:T(8,128)(2,1)S(1)} %bitcast.97), channel_id=1, source_target_pairs={{0,8},{8,16},{16,24},{24,32},{32,40},{40,48},{48,56},{56,64},{64,7... | collective-permute-start | bytes 786440 | tf_op jit(solution)/shard_map/ppermute | solution.py:25
  16.1 12.1 %collective-permute-start = (bf16[1024,128]{0,1:T(8,128)(2,1)S(1)}, bf16[1024,128]{0,1:T(8,128)(2,1)S(1)}, u32[]{:S(2)}, u32[]{:S(2)}) collective-permute-start(bf16[1024,128]{0,1:T(8,128)(2,1)S(1)} %bitcast.98), channel_id=1, source_target_pairs={{0,16},{8,24},{16,32},{24,40},{32,48},{40,56},{48,64},{56,72},{64,... | collective-permute-start | bytes 786440 | tf_op jit(solution)/shard_map/ppermute | solution.py:25
  28.2 37.7 %copy-start.2 = (bf16[256,2048]{1,0:T(8,128)(2,1)S(1)}, bf16[256,2048]{1,0:T(8,128)(2,1)}, u32[]{:S(2)}) copy-start(bf16[256,2048]{1,0:T(8,128)(2,1)} %param.12) | copy-start | bytes 3145732
  65.9 3.4 copy-start.3
  69.2 20.4 %copy-start.4 = (s32[2048]{0:T(1024)S(1)}, s32[2048]{0:T(1024)}, u32[]{:S(2)}) copy-start(s32[2048]{0:T(1024)} %param.15) | copy-start | bytes 24580
  72.8 16.8 %all-to-all-start = ((bf16[32,4,1024]{2,1,0:T(4,128)(2,1)}), bf16[32,4,1024]{2,1,0:T(4,128)(2,1)S(1)}, u32[]{:S(2)}, u32[]{:S(2)}) async-start(bf16[32,4,1024]{2,1,0:T(4,128)(2,1)} %reshape.133), calls=%async_computation | async-start | bytes 524288 | tf_op jit(solution)/shard_map/all_to_all | solution.py:89
  364.6 16.2 %copy-start.1 = (bf16[2048,512]{1,0:T(8,128)(2,1)S(1)}, bf16[2048,512]{1,0:T(8,128)(2,1)}, u32[]{:S(2)}) copy-start(bf16[2048,512]{1,0:T(8,128)(2,1)} %param.11) | copy-start | bytes 6291460
Sparse Core Ops, SparseCore 0:
  69.4 295.1 all-gather.2
